TPU v7x, 32 devices: a whole 2x2x4 slice. The times are simulated.
32 devices in a mesh: px: 4 (over y, x), py: 8 (over z, core).
Axes of the slice: x: 2, y: 2, z: 4, core: 2. Of those that a mesh axis runs over, the one named last changes fastest.
Arguments:
- residual: float32 [10, 2048, 2048], P(None, 'py', 'px'), may hold values from -6 to 6
- lambda_x: float32 [2048], P('px'), may hold values from 0.1 to 4
- lambda_y: float32 [2048], P('py'), may hold values from 0.1 to 4
- coupling: float32 [9], replicated, may hold values from 0.2 to 2
- layer_shift: float32 [10], replicated, may hold values from 0.05 to 1
- left_x: bfloat16 [2048, 2048], P(None, 'px'), may hold values from -0.125 to 0.125
- left_y: bfloat16 [2048, 2048], P('py'), may hold values from -0.125 to 0.125
- right_y: bfloat16 [2048, 2048], P('py'), may hold values from -0.125 to 0.125
- right_x: bfloat16 [2048, 2048], P(None, 'px'), may hold values from -0.125 to 0.125
- regime_code: int32 [10, 2048, 2048], P(None, 'py', 'px'), may hold values from 0 to 3
- upwind_flag: int32 [2, 10, 2048, 2048], P(None, None, 'py', 'px'), may hold values from 0 to 1
- mobility_table: float32 [4], replicated, may hold values from 0.3 to 3
Outputs:
- correction: float32 [10, 2048, 2048], P(None, 'py', 'px')
- balance: float32 [10, 2048, 2048], P(None, 'py', 'px')
Inputs may be any that keep to these rules, and one draw needn't show every extreme that they name: `regime_code`: a regime number of each cell.
All inputs are finite; a program needn't handle non-finite values.
Results may differ from a plain program's by a relative error of at most 0.0057.
Values may be sent and summed in bfloat16 or wider, within the bound.
No kernel may reach another device: no remote copies, remote signals or barrier semaphores. Data moves between devices by JAX's collectives and lax.ppermute only.
A program may use at most 192 MiB of HBM per device.

v0:
```python
import jax
import jax.numpy as jnp
from jax import lax
from jax.sharding import PartitionSpec as P


def with_halo(block, sides, width):
    for axis, dim in sides:
        count = lax.axis_size(axis)
        forward = [(i, i + 1) for i in range(count - 1)]
        backward = [(target, source) for source, target in forward]
        low = lax.ppermute(
            lax.slice_in_dim(block, block.shape[dim] - width, None, axis=dim), axis, forward
        )
        high = lax.ppermute(lax.slice_in_dim(block, 0, width, axis=dim), axis, backward)
        block = jnp.concatenate([low, block, high], axis=dim)
    return block


def thomas_solve(rhs, lambda_x, lambda_y, coupling, layer_shift):
    layers = rhs.shape[0]
    mode_sum = lambda_y[:, None] + lambda_x[None, :]
    ratios = []
    partial_values = []
    for layer_index in range(layers):
        diagonal = mode_sum + layer_shift[layer_index]
        if layer_index > 0:
            diagonal = diagonal + coupling[layer_index - 1]
        if layer_index < layers - 1:
            diagonal = diagonal + coupling[layer_index]
        if layer_index == 0:
            pivots = diagonal
            solved = rhs[0] / pivots
        else:
            pivots = diagonal + coupling[layer_index - 1] * ratios[-1]
            solved = (rhs[layer_index] + coupling[layer_index - 1] * partial_values[-1]) / pivots
        partial_values.append(solved)
        if layer_index < layers - 1:
            ratios.append(-coupling[layer_index] / pivots)
    results = [partial_values[layers - 1]]
    for layer_index in range(layers - 2, -1, -1):
        results.append(partial_values[layer_index] - ratios[layer_index] * results[-1])
    return jnp.stack(results[::-1])


def shards(
    residual,
    lambda_x,
    lambda_y,
    coupling,
    layer_shift,
    left_x,
    left_y,
    right_y,
    right_x,
    regime_code,
    upwind_flag,
    mobility_table,
):
    count_y = lax.axis_size("py")
    rounded = residual.astype(jnp.bfloat16)
    spectral_x = jnp.einsum(
        "zyx,xi->zyi",
        lax.all_gather(rounded, "px", axis=2, tiled=True),
        left_x,
        preferred_element_type=jnp.float32,
    ).astype(jnp.bfloat16)
    pencil = lax.all_to_all(spectral_x, "py", 2, 1, tiled=True)
    modes = pencil.shape[2]
    spectral = jnp.einsum(
        "jy,zyi->zji",
        lax.all_gather(left_y, "py", axis=0, tiled=True),
        pencil,
        preferred_element_type=jnp.float32,
    )
    own_x = lax.dynamic_slice_in_dim(lambda_x, lax.axis_index("py") * modes, modes)
    all_y = lax.all_gather(lambda_y, "py", axis=0, tiled=True)
    solved = thomas_solve(spectral, own_x, all_y, coupling, layer_shift).astype(jnp.bfloat16)
    back_pencil = jnp.einsum(
        "yj,zji->zyi",
        lax.all_gather(right_y, "py", axis=0, tiled=True),
        solved,
        preferred_element_type=jnp.float32,
    ).astype(jnp.bfloat16)
    back_y = lax.all_to_all(back_pencil, "py", 1, 2, tiled=True)
    del count_y
    mobility = jnp.zeros(regime_code.shape, jnp.float32)
    for regime in range(mobility_table.shape[0]):
        mobility = jnp.where(regime_code == regime, mobility_table[regime], mobility)
    correction = jnp.einsum(
        "zyi,ix->zyx",
        lax.all_gather(back_y, "px", axis=2, tiled=True),
        right_x,
        preferred_element_type=jnp.float32,
    )
    width_x = correction.shape[2]
    width_y = correction.shape[1]
    stacked = jnp.stack(
        [
            correction,
            mobility,
            upwind_flag[0].astype(jnp.float32),
            upwind_flag[1].astype(jnp.float32),
        ]
    )
    extended = with_halo(stacked, (("px", 3), ("py", 2)), 1)
    press_x = extended[0][:, 1:-1, :]
    mobil_x = extended[1][:, 1:-1, :]
    flags_x = extended[2][:, 1:-1, :]
    upwind_x = jnp.where(flags_x[:, :, :-1] > 0.5, mobil_x[:, :, :-1], mobil_x[:, :, 1:])
    flux_x = upwind_x * (press_x[:, :, :-1] - press_x[:, :, 1:])
    faces_x = lax.axis_index("px") * width_x + jnp.arange(width_x + 1, dtype=jnp.int32)
    valid_x = (faces_x >= 1) & (faces_x <= width_x * lax.axis_size("px") - 1)
    flux_x = jnp.where(valid_x[None, None, :], flux_x, 0.0)
    net_x = flux_x[:, :, 1:] - flux_x[:, :, :-1]
    press_y = extended[0][:, :, 1:-1]
    mobil_y = extended[1][:, :, 1:-1]
    flags_y = extended[3][:, :, 1:-1]
    upwind_y = jnp.where(flags_y[:, :-1, :] > 0.5, mobil_y[:, :-1, :], mobil_y[:, 1:, :])
    flux_y = upwind_y * (press_y[:, :-1, :] - press_y[:, 1:, :])
    faces_y = lax.axis_index("py") * width_y + jnp.arange(width_y + 1, dtype=jnp.int32)
    valid_y = (faces_y >= 1) & (faces_y <= width_y * lax.axis_size("py") - 1)
    flux_y = jnp.where(valid_y[None, :, None], flux_y, 0.0)
    net_y = flux_y[:, 1:, :] - flux_y[:, :-1, :]
    balance = net_x + net_y
    return (correction, balance)


def solution(mesh):
    return jax.shard_map(
        shards,
        mesh=mesh,
        in_specs=(
            P(None, "py", "px"),
            P("px"),
            P("py"),
            P(),
            P(),
            P(None, "px"),
            P("py", None),
            P("py", None),
            P(None, "px"),
            P(None, "py", "px"),
            P(None, None, "py", "px"),
            P(),
        ),
        out_specs=(P(None, "py", "px"), P(None, "py", "px")),
        check_vma=False,
    )
```

profile of v0, /device:TPU:3, one launch (start us, length us, event | category | flops | bytes accessed | tf_op | source)
XLA Modules:
  0.0 748.3 jit_solution(3291203513705140137)
XLA Ops:
  7.2 4.5 convert_element_type.21
  13.2 104.8 %all-gather.6.cloned.1.call-done = bf16[10,256,2048]{2,1,0:T(8,128)(2,1)} async-done(((bf16[10,256,512]{2,1,0:T(8,128)(2,1)}), bf16[10,256,2048]{2,1,0:T(8,128)(2,1)}) %all-gather.6.cloned.1.call-update) | async-done | bytes 10485776 | tf_op jit(solution)/shard_map/all_gather | solution.py:64
  118.0 10.8 %fusion.22 = bf16[10,256,512]{2,1,0:T(8,128)(2,1)} fusion(bf16[10,256,2048]{2,1,0:T(8,128)(2,1)} %all-gather.6.cloned.1.call-done, bf16[2048,512]{1,0:T(8,128)(2,1)S(1)} %copy-done), kind=kOutput, calls=%fused_computation.46 | convolution fusion | flops 5370019840 | bytes 15204352 | tf_op jit(solution)/shard_map/zyx,xi->zyi/dot_general | solution.py:62
  128.9 7.6 %copy.29 = bf16[10,256,512]{1,0,2:T(8,128)(2,1)} copy(bf16[10,256,512]{2,1,0:T(8,128)(2,1)} %fusion.22) | data formatting | bytes 5242880 | tf_op jit(solution)/shard_map/convert_element_type | solution.py:67
  136.5 5.5 all-to-all-start
  148.2 0.8 dynamic_slice.3
  149.0 121.9 %all-gather = f32[8,1,256]{2,1,0:T(1,128)S(1)} all-gather(f32[1,1,256]{2,1,0:T(1,128)S(1)} %bitcast.92), channel_id=1, replica_groups=mesh['px'=4,'py'=8] {'py'}, dimensions={0}, use_global_device_ids=true | all-gather | bytes 9216 | tf_op jit(solution)/shard_map/all_gather | solution.py:77
  271.5 26.8 %all-to-all-done = bf16[10,256,512]{1,0,2:T(8,128)(2,1)} async-done(((bf16[10,256,512]{1,0,2:T(8,128)(2,1)}), bf16[10,256,512]{1,0,2:T(8,128)(2,1)}, u32[]{:S(2)}, u32[]{:S(2)}) %all-to-all-start) | async-done | bytes 2621472 | tf_op jit(solution)/shard_map/all_to_all | solution.py:68
  298.4 5.3 copy.31
  303.7 5.7 all_to_all.29
  309.4 9.0 %fusion.9 = f32[10,2048,64]{1,2,0:T(8,128)S(1)} fusion(bf16[10,2048,64]{1,2,0:T(8,128)(2,1)} %all_to_all.29, bf16[2048,2048]{1,0:T(8,128)(2,1)} %all-gather.8.cloned.1.call-done), kind=kOutput, calls=%fused_computation.29 | convolution fusion | flops 5368709120 | bytes 16252928 | tf_op jit(solution)/shard_map/jy,zyi->zji/dot_general | solution.py:70
  318.4 14.9 %fusion.70 = (bf16[10,2048,64]{1,2,0:T(8,128)(2,1)}, bf16[1,2048,64]{1,2,0:T(8,128)(2,1)S(1)}, f32[1,2048,64]{1,2,0:T(8,128)S(1)}, f32[1,2048,64]{1,2,0:T(8,128)...) fusion(f32[]{:T(128)S(6)} %neg.27, f32[]{:T(128)} %bitcast.9, ...), kind=kLoop, calls=%fused_computation.110 | loop fusion | flops 13631487 | bytes 8921456
  334.1 4.8 convert_dynamic-update-slice_fusion.7
  338.9 0.7 convert_dynamic-update-slice_fusion.6
  339.6 7.6 %convert_dynamic-update-slice_fusion.5 = bf16[10,2048,64]{1,2,0:T(8,128)(2,1)} fusion(bf16[10,2048,64]{1,2,0:T(8,128)(2,1)} %convert_dynamic-update-slice_fusion.6, f32[1,2048,64]{1,2,0:T(8,128)S(1)} %get-tuple-element.8, f32[1,2048,64]{1,2,0:T(8,128)S(1)} %get-tuple-element.5, f32[]{:T(128)} %bitcast.8, f32[]{:T(128)S(6)} %neg.27, f32[]{:T(128)} %bitcast.9, ...), kind=kLoop, calls=%fused_computation.116 | loop fusion | flops 4063232 | bytes 1324308
  347.2 0.7 convert_dynamic-update-slice_fusion.4
  348.0 10.4 %convert_dynamic-update-slice_fusion.3 = bf16[10,2048,64]{1,2,0:T(8,128)(2,1)} fusion(bf16[10,2048,64]{1,2,0:T(8,128)(2,1)} %convert_dynamic-update-slice_fusion.4, f32[1,2048,64]{1,2,0:T(8,128)S(1)} %get-tuple-element.7, f32[1,2048,64]{1,2,0:T(8,128)S(1)} %get-tuple-element.6, f32[]{:T(128)} %bitcast.8, f32[]{:T(128)S(6)} %neg.27, f32[]{:T(128)} %bitcast.9, ...), kind=kLoop, calls=%fused_computation.114 | loop fusion | flops 5636096 | bytes 1326364
  358.4 0.7 convert_dynamic-update-slice_fusion.2
  359.1 14.0 %convert_dynamic-update-slice_fusion.1 = bf16[10,2048,64]{1,2,0:T(8,128)(2,1)} fusion(bf16[10,2048,64]{1,2,0:T(8,128)(2,1)} %convert_dynamic-update-slice_fusion.2, f32[]{:T(128)} %bitcast.8, f32[]{:T(128)S(6)} %neg.27, f32[]{:T(128)} %bitcast.9, f32[]{:T(128)} %bitcast.10, f32[]{:T(128)S(6)} %neg.28, f32[]{:T(128)} %bitcast.11, f32[]{:T(128)} %bitcast.12, ...), kind=kLoop, calls=%fused_computation.112 | loop fusion | flops 8912896 | bytes 2377508
  373.1 14.0 %convert_dynamic-update-slice_fusion = bf16[10,2048,64]{1,2,0:T(8,128)(2,1)} fusion(bf16[10,2048,64]{1,2,0:T(8,128)(2,1)} %convert_dynamic-update-slice_fusion.1, f32[]{:T(128)} %bitcast.8, f32[]{:T(128)S(6)} %neg.27, f32[]{:T(128)} %bitcast.9, f32[]{:T(128)} %bitcast.10, f32[]{:T(128)S(6)} %neg.28, f32[]{:T(128)} %bitcast.11, f32[]{:T(128)} %bitcast.12, ...), kind=kLoop, calls=%fused_computation.111 | loop fusion | flops 8650752 | bytes 2377508 | tf_op jit(solution)/shard_map/stack | solution.py:43
  387.1 10.7 %fusion.15 = bf16[10,2048,64]{1,2,0:T(8,128)(2,1)} fusion(bf16[10,2048,64]{1,2,0:T(8,128)(2,1)} %convert_dynamic-update-slice_fusion, bf16[2048,2048]{1,0:T(8,128)(2,1)} %all-gather.10.cloned.1.call-done), kind=kOutput, calls=%fused_computation.31 | convolution fusion | flops 5370019840 | bytes 13631488 | tf_op jit(solution)/shard_map/yj,zji->zyi/dot_general | solution.py:79
  397.8 10.4 %copy.32 = bf16[10,2048,64]{2,0,1:T(8,128)(2,1)} copy(bf16[10,2048,64]{1,2,0:T(8,128)(2,1)} %fusion.15) | data formatting | bytes 5242880 | tf_op jit(solution)/shard_map/convert_element_type | solution.py:84
  408.2 9.0 %reshape.799 = bf16[8,2,81920]{2,1,0:T(2,128)(2,1)} reshape(bf16[2048,10,64]{2,1,0:T(8,128)(2,1)} %bitcast.83) | data formatting | bytes 5242880
  417.2 66.5 %all_to_all.36 = bf16[8,2,81920]{2,1,0:T(2,128)(2,1)} all-to-all(bf16[8,2,81920]{2,1,0:T(2,128)(2,1)} %reshape.799), channel_id=1, replica_groups=mesh['px'=4,'py'=8] {'py'}, dimensions={0} | all-to-all | bytes 5242880 | tf_op jit(solution)/shard_map/all_to_all | solution.py:85
  483.7 8.9 %reshape.800 = bf16[2048,10,64]{2,1,0:T(8,128)(2,1)} reshape(bf16[8,2,81920]{2,1,0:T(2,128)(2,1)} %all_to_all.36) | data formatting | bytes 5242880
  492.6 9.1 %copy.34 = bf16[10,256,8,64]{1,3,2,0:T(8,128)(2,1)} copy(bf16[10,256,8,64]{3,0,1,2:T(8,128)(2,1)} %bitcast.84) | data formatting | bytes 5242880 | tf_op jit(solution)/shard_map/all_to_all | solution.py:85
  501.7 4.4 copy.35
  506.8 9.1 %select_bitcast_fusion = f32[1,10,256,512]{3,2,1,0:T(8,128)} fusion(s32[10,256,512]{2,1,0:T(8,128)} %param.21, f32[]{:T(128)} %bitcast.38, f32[]{:T(128)} %bitcast.37, f32[]{:T(128)} %bitcast.36, f32[]{:T(128)} %bitcast.35), kind=kLoop, calls=%fused_computation.28 | loop fusion | flops 10485760 | bytes 10485776 | tf_op jit(solution)/shard_map/stack | solution.py:98
  515.8 10.4 %slice_convert_fusion.1 = (f32[1,10,256,512]{3,2,1,0:T(8,128)}, f32[1,10,256,512]{3,2,1,0:T(8,128)}) fusion(s32[2,10,256,512]{3,2,1,0:T(8,128)} %param.22), kind=kLoop, calls=%fused_computation.27 | loop fusion | flops 2621440 | bytes 20971520 | tf_op jit(solution)/shard_map/convert_element_type | solution.py:102
  526.2 83.4 %all-gather.12.cloned.1.call-done = bf16[10,256,2048]{2,1,0:T(8,128)(2,1)} async-done(((bf16[10,256,512]{2,1,0:T(8,128)(2,1)}), bf16[10,256,2048]{2,1,0:T(8,128)(2,1)}) %all-gather.12.cloned.1.call-update) | async-done | bytes 10485776 | tf_op jit(solution)/shard_map/all_gather | solution.py:92
  609.6 8.5 %fusion.18 = f32[10,256,512]{2,1,0:T(8,128)S(1)} fusion(bf16[10,256,2048]{2,1,0:T(8,128)(2,1)} %all-gather.12.cloned.1.call-done, bf16[2048,512]{1,0:T(8,128)(2,1)S(1)} %copy-done.14), kind=kOutput, calls=%fused_computation.42 | convolution fusion | flops 5368709120 | bytes 17825792 | tf_op jit(solution)/shard_map/zyi,ix->zyx/dot_general | solution.py:90
  618.2 5.9 pad_maximum_fusion.4
  624.1 3.3 copy.36
  627.4 3.1 collective-permute-start
  630.6 3.3 copy.37
  633.9 2.2 collective-permute-start.1
  636.1 3.2 copy.38
  639.5 3.1 copy.39
  642.6 2.3 pad_maximum_fusion.10
  644.9 5.4 collective-permute-start.2
  650.3 1.9 collective-permute-start.3
  652.2 4.0 collective-permute-done.3
  656.3 27.9 %pad_maximum_fusion = f32[4,10,258,514]{3,2,1,0:T(8,128)} fusion(f32[4,10,1,514]{3,2,1,0:T(1,128)S(1)} %collective-permute-done.3, f32[4,10,256,1]{3,2,1,0:T(8,128)S(1)} %copy-done.8, f32[1,10,256,512]{3,2,1,0:T(8,128)} %get-tuple-element.19, f32[1,10,256,512]{3,2,1,0:T(8,128)S(1)} %bitcast.79, f32[1,10,256,512]{3,2,1,0:T(8,128)} %select_bitcast_fusion, ...), kind=kLoop, calls=%fused_computation | loop fusion | flops 37131360 | bytes 42435840 | tf_op jit(solution)/shard_map/concatenate | solution.py:16
  684.2 18.6 %slice_bitcast_fusion.3 = (f32[10,258,514]{2,1,0:T(8,128)}, f32[10,258,514]{2,1,0:T(8,128)}, f32[10,258,514]{2,1,0:T(8,128)}, f32[10,258,514]{2,1,0:T(8,128)}) fusion(f32[4,10,258,514]{3,2,1,0:T(8,128)} %pad_maximum_fusion), kind=kLoop, calls=%fused_computation.8 | loop fusion | bytes 42435840 | tf_op jit(solution)/shard_map/squeeze | solution.py:109
  702.7 14.9 %fusion.5 = f32[10,256,513]{2,1,0:T(8,128)} fusion(f32[10,258,514]{2,1,0:T(8,128)} %get-tuple-element.14, f32[10,258,514]{2,1,0:T(8,128)} %get-tuple-element.15, f32[10,258,514]{2,1,0:T(8,128)} %get-tuple-element.12, pred[513]{0:T(1024)(128)(4,1)S(1)} %fusion.73), kind=kLoop, calls=%fused_computation.11 | loop fusion | flops 6566400 | bytes 31519232 | tf_op jit(solution)/shard_map/jit(_where)/select_n | solution.py:114
  717.7 1.9 copy-done.3
  719.6 10.7 %fusion.7 = f32[10,257,512]{2,1,0:T(8,128)} fusion(f32[10,258,514]{2,1,0:T(8,128)S(1)} %copy-done.2, f32[10,258,514]{2,1,0:T(8,128)S(1)} %copy-done.3, f32[10,258,514]{2,1,0:T(8,128)} %get-tuple-element.13, pred[257]{0:T(512)(128)(4,1)S(1)} %fusion.76), kind=kLoop, calls=%fused_computation.16 | loop fusion | flops 6579200 | bytes 31580416 | tf_op jit(solution)/shard_map/jit(_where)/select_n | solution.py:123
  730.3 11.2 %fusion.8 = f32[10,256,512]{2,1,0:T(8,128)} fusion(f32[10,257,512]{2,1,0:T(8,128)} %fusion.7, f32[10,256,513]{2,1,0:T(8,128)} %fusion.5), kind=kLoop, calls=%fused_computation.20 | loop fusion | flops 3932160 | bytes 26214400 | tf_op jit(solution)/shard_map/add | solution.py:125
  (53 shorter events, 4.7 us)
Async XLA Ops:
  7.2 110.8 %copy-start = (bf16[2048,512]{1,0:T(8,128)(2,1)S(1)}, bf16[2048,512]{1,0:T(8,128)(2,1)}, u32[]{:S(2)}) copy-start(bf16[2048,512]{1,0:T(8,128)(2,1)} %param.17) | copy-start | bytes 6291460
  7.2 110.8 %all-gather.6.cloned.1.call-start = ((), (), s32[]{:S(2)}) async-start(), calls=%async_computation.2 | async-start | bytes 13107200 | tf_op jit(solution)/shard_map/all_gather | solution.py:64
  11.7 297.7 %all-gather.8.cloned.1.call-start = ((), (), s32[]{:S(2)}) async-start(), calls=%async_computation.3 | async-start | bytes 9437184 | tf_op jit(solution)/shard_map/all_gather | solution.py:72
  12.5 374.6 %all-gather.10.cloned.1.call-start = ((), (), s32[]{:S(2)}) async-start(), calls=%async_computation.4 | async-start | bytes 9437184 | tf_op jit(solution)/shard_map/all_gather | solution.py:81
  136.5 5.5 copy-start.11
  136.5 12.5 %copy-start.13 = (f32[256]{0:T(256)S(1)}, f32[256]{0:T(256)}, u32[]{:S(2)}) copy-start(f32[256]{0:T(256)} %param.14) | copy-start | bytes 3076
  136.5 134.4 %copy-start.10 = (f32[10]{0:T(128)S(1)}, f32[10]{0:T(128)}, u32[]{:S(2)}) copy-start(f32[10]{0:T(128)} %param.16) | copy-start | bytes 124
  136.5 161.9 %all-to-all-start = ((bf16[10,256,512]{1,0,2:T(8,128)(2,1)}), bf16[10,256,512]{1,0,2:T(8,128)(2,1)}, u32[]{:S(2)}, u32[]{:S(2)}) async-start(bf16[10,256,512]{1,0,2:T(8,128)(2,1)} %copy.29), calls=%async_computation | async-start | bytes 8388608 | tf_op jit(solution)/shard_map/all_to_all | solution.py:68
  142.0 467.6 %all-gather.12.cloned.1.call-start = ((), (), s32[]{:S(2)}) async-start(), calls=%async_computation.5 | async-start | bytes 13107200 | tf_op jit(solution)/shard_map/all_gather | solution.py:92
  501.7 4.4 copy-start.12
  515.8 93.8 %copy-start.14 = (bf16[2048,512]{1,0:T(8,128)(2,1)S(1)}, bf16[2048,512]{1,0:T(8,128)(2,1)}, u32[]{:S(2)}) copy-start(bf16[2048,512]{1,0:T(8,128)(2,1)} %param.20) | copy-start | bytes 6291460
  609.6 8.5 %copy-start.4 = (f32[1,10,256,512]{3,2,1,0:T(8,128)S(1)}, f32[1,10,256,512]{3,2,1,0:T(8,128)}, u32[]{:S(2)}) copy-start(f32[1,10,256,512]{3,2,1,0:T(8,128)} %get-tuple-element.18) | copy-start | bytes 15728644
  609.6 8.5 %copy-start.5 = (f32[1,10,256,512]{3,2,1,0:T(8,128)S(1)}, f32[1,10,256,512]{3,2,1,0:T(8,128)}, u32[]{:S(2)}) copy-start(f32[1,10,256,512]{3,2,1,0:T(8,128)} %get-tuple-element.19) | copy-start | bytes 15728644
  609.6 8.6 %copy-start.6 = (f32[1,10,256,512]{3,2,1,0:T(8,128)S(1)}, f32[1,10,256,512]{3,2,1,0:T(8,128)}, u32[]{:S(2)}) copy-start(f32[1,10,256,512]{3,2,1,0:T(8,128)} %select_bitcast_fusion) | copy-start | bytes 15728644
  618.1 6.0 copy-start.9
  627.4 8.6 %collective-permute-start = (f32[4,10,256,1]{2,0,3,1:T(4,128)S(1)}, f32[4,10,256,1]{2,0,3,1:T(4,128)S(1)}, u32[]{:S(2)}, u32[]{:S(2)}) collective-permute-start(f32[4,10,256,1]{2,0,3,1:T(4,128)S(1)} %copy.36), channel_id=1, source_target_pairs={{0,8},{8,16},{16,24},{1,9},{9,17},{17,25},{2,10},{10,18},{18,26},{... | collective-permute-start | bytes 122888 | tf_op jit(solution)/shard_map/ppermute | solution.py:12
  633.9 5.6 collective-permute-start.1
  639.5 16.8 %slice-start = ((s8[5242880]{0:T(1024)(128)(4,1)}), s8[1048576]{0:T(1024)(128)(4,1)S(1)}, s32[]{:S(2)}) async-start(s8[5242880]{0:T(1024)(128)(4,1)} %bitcast.78), calls=%async_computation.6 | async-start | bytes 2097152
  642.6 13.7 %slice-start.1 = ((s8[5242880]{0:T(1024)(128)(4,1)}), s8[4194304]{0:T(1024)(128)(4,1)S(1)}, s32[]{:S(2)}) async-start(s8[5242880]{0:T(1024)(128)(4,1)} %bitcast.78), calls=%async_computation.7 | async-start | bytes 8388608
  642.6 13.7 %copy-start.7 = (f32[4,10,256,1]{3,2,1,0:T(8,128)S(1)}, f32[4,10,256,1]{3,2,1,0:T(8,128)}, u32[]{:S(2)}) copy-start(f32[4,10,256,1]{3,2,1,0:T(8,128)} %copy.38) | copy-start | bytes 122884
  642.6 13.7 %copy-start.8 = (f32[4,10,256,1]{3,2,1,0:T(8,128)S(1)}, f32[4,10,256,1]{3,2,1,0:T(8,128)}, u32[]{:S(2)}) copy-start(f32[4,10,256,1]{3,2,1,0:T(8,128)} %copy.39) | copy-start | bytes 122884
  644.9 7.3 collective-permute-start.2
  650.3 6.0 collective-permute-start.3
  702.7 14.9 %copy-start.2 = (f32[10,258,514]{2,1,0:T(8,128)S(1)}, f32[10,258,514]{2,1,0:T(8,128)}, u32[]{:S(2)}) copy-start(f32[10,258,514]{2,1,0:T(8,128)} %get-tuple-element.14) | copy-start | bytes 15913444
  702.7 16.9 %copy-start.3 = (f32[10,258,514]{2,1,0:T(8,128)S(1)}, f32[10,258,514]{2,1,0:T(8,128)}, u32[]{:S(2)}) copy-start(f32[10,258,514]{2,1,0:T(8,128)} %get-tuple-element.15) | copy-start | bytes 15913444
  730.3 11.2 %copy-start.1 = (bf16[2048,512]{1,0:T(8,128)(2,1)S(1)}, bf16[2048,512]{1,0:T(8,128)(2,1)}, u32[]{:S(2)}) copy-start(bf16[2048,512]{1,0:T(8,128)(2,1)} %param.17) | copy-start | bytes 6291460
Sparse Core Ops, SparseCore 0:
  11.8 106.1 all-gather.5
  119.6 155.0 all-gather.7
  276.3 83.3 all-gather.9
  506.2 103.3 all-gather.11
where the time goes:
time: 755 us; the launch traced here: 748 us
  waiting for transfers between devices  221 us (29%)
  blocking collectives  188 us (25%)
  other arithmetic  165 us (22%)
  local copies, waits for them, and re-layouts  97.4 us (13%)
  matrix products  39.1 us (5%)
  between operations  19.7 us (3%)
  starting transfers between devices  18.2 us (2%)
    all_gather x1, blocking collectives, shards(): all_y = lax.all_gather(lambda_y, 'py', axis=0, tiled=True)  122 us
    all_gather x1, waiting for transfers between devices, shards(): lax.all_gather(rounded, 'px', axis=2, tiled=True)  105 us
    all_gather x1, waiting for transfers between devices, shards(): lax.all_gather(back_y, 'px', axis=2, tiled=True)  83.4 us
    all_to_all x1, blocking collectives, shards(): back_y = lax.all_to_all(back_pencil, 'py', 1, 2, tiled=True)  66.5 us
    unnamed x9, other arithmetic  54 us
    concatenate x1, other arithmetic, with_halo(): block = jnp.concatenate([low, block, high], axis=dim)  27.9 us
    all_to_all x1, waiting for transfers between devices, shards(): pencil = lax.all_to_all(spectral_x, 'py', 2, 1, tiled=True)  26.8 us
    unnamed x37, local copies, waits for them, and re-layouts  20.7 us
  transfers between devices with their start and end apart: 9, of which 5 were waited for; matrix products, arithmetic and copies ran while one was open for 17% of the time, Pallas kernels for 0%

commit v1 on v0

--- a/solution.py
+++ b/solution.py
@@ -82,7 +82,15 @@
         solved,
         preferred_element_type=jnp.float32,
     ).astype(jnp.bfloat16)
-    back_y = lax.all_to_all(back_pencil, "py", 1, 2, tiled=True)
+    back_y = jnp.concatenate(
+        lax.all_to_all(
+            jnp.stack(jnp.split(back_pencil, lax.axis_size("py"), 1)),
+            axis_name="py",
+            concat_axis=0,
+            split_axis=0,
+        ),
+        2,
+    )
     del count_y
     mobility = jnp.zeros(regime_code.shape, jnp.float32)
     for regime in range(mobility_table.shape[0]):

time: 755 us -> 718 us (0.951)
  local copies, waits for them, and re-layouts: 97.4 us -> 62.2 us
    unnamed x37 -> x42, local copies, waits for them, and re-layouts: 20.7 us -> 3.11 us
    all_to_all x2 -> x0, local copies, waits for them, and re-layouts: 13.4 us -> none  [shards(): back_y = lax.all_to_all(back_pencil, 'py', 1, 2, tiled=True)]
    convert_element_type x1 -> x0, local copies, waits for them, and re-layouts: 10.4 us -> none  [shards(): back_pencil = jnp.einsum('yj,zji->zyi', lax.all_gather(right_y, 'py', axi...]
  transfers between devices with their start and end apart: 9 -> 9, of which waited for: 5 -> 5; matrix products, arithmetic and copies ran while one was open for 17% -> 18% of each run, Pallas kernels for 0% -> 0%
where the time goes in v1:
time: 718 us; the launch traced here: 712 us
  waiting for transfers between devices  221 us (31%)
  blocking collectives  187 us (26%)
  other arithmetic  165 us (23%)
  local copies, waits for them, and re-layouts  62.2 us (9%)
  matrix products  38.2 us (5%)
  between operations  19.8 us (3%)
  starting transfers between devices  18.2 us (3%)
    all_gather x1, blocking collectives, shards(): all_y = lax.all_gather(lambda_y, 'py', axis=0, tiled=True)  122 us
    all_gather x1, waiting for transfers between devices, shards(): lax.all_gather(rounded, 'px', axis=2, tiled=True)  105 us
    all_gather x1, waiting for transfers between devices, shards(): lax.all_gather(back_y, 'px', axis=2, tiled=True)  83.9 us
    all_to_all x1, blocking collectives, shards(): lax.all_to_all(jnp.stack(jnp.split(back_pencil, lax.axis_size('py'), 1)),...  65.4 us
    unnamed x9, other arithmetic  54 us
    concatenate x1, other arithmetic, with_halo(): block = jnp.concatenate([low, block, high], axis=dim)  27.9 us
    all_to_all x1, waiting for transfers between devices, shards(): pencil = lax.all_to_all(spectral_x, 'py', 2, 1, tiled=True)  26.8 us
    squeeze x1, local copies, waits for them, and re-layouts, shards(): flags_x = extended[2][:, 1:-1, :]  18.6 us
  transfers between devices with their start and end apart: 9, of which 5 were waited for; matrix products, arithmetic and copies ran while one was open for 18% of the time, Pallas kernels for 0%

profile of v1, /device:TPU:3, one launch (start us, length us, event | category | flops | bytes accessed | tf_op | source)
XLA Modules:
  0.0 712.0 jit_solution(6561292869936975260)
XLA Ops:
  7.2 4.5 convert_element_type.21
  11.8 0.7 all-gather.8.cloned.1.call-update
  13.2 104.8 %all-gather.6.cloned.1.call-done = bf16[10,256,2048]{2,1,0:T(8,128)(2,1)} async-done(((bf16[10,256,512]{2,1,0:T(8,128)(2,1)}), bf16[10,256,2048]{2,1,0:T(8,128)(2,1)}) %all-gather.6.cloned.1.call-update) | async-done | bytes 10485776 | tf_op jit(solution)/shard_map/all_gather | solution.py:64
  118.0 10.8 %fusion.22 = bf16[10,256,512]{2,1,0:T(8,128)(2,1)} fusion(bf16[10,256,2048]{2,1,0:T(8,128)(2,1)} %all-gather.6.cloned.1.call-done, bf16[2048,512]{1,0:T(8,128)(2,1)S(1)} %copy-done), kind=kOutput, calls=%fused_computation.46 | convolution fusion | flops 5370019840 | bytes 15204352 | tf_op jit(solution)/shard_map/zyx,xi->zyi/dot_general | solution.py:62
  128.9 7.6 %copy.19 = bf16[10,256,512]{1,0,2:T(8,128)(2,1)} copy(bf16[10,256,512]{2,1,0:T(8,128)(2,1)} %fusion.22) | data formatting | bytes 5242880 | tf_op jit(solution)/shard_map/convert_element_type | solution.py:67
  136.5 5.5 all-to-all-start
  142.0 0.7 fusion.90
  148.2 0.8 dynamic_slice.3
  149.0 121.9 %all-gather = f32[8,1,256]{2,1,0:T(1,128)S(1)} all-gather(f32[1,1,256]{2,1,0:T(1,128)S(1)} %bitcast.118), channel_id=1, replica_groups=mesh['px'=4,'py'=8] {'py'}, dimensions={0}, use_global_device_ids=true | all-gather | bytes 9216 | tf_op jit(solution)/shard_map/all_gather | solution.py:77
  271.5 26.8 %all-to-all-done = bf16[10,256,512]{1,0,2:T(8,128)(2,1)} async-done(((bf16[10,256,512]{1,0,2:T(8,128)(2,1)}), bf16[10,256,512]{1,0,2:T(8,128)(2,1)}, u32[]{:S(2)}, u32[]{:S(2)}) %all-to-all-start) | async-done | bytes 2621472 | tf_op jit(solution)/shard_map/all_to_all | solution.py:68
  298.4 5.3 copy.21
  303.7 5.7 all_to_all.19
  309.4 9.0 %fusion.9 = f32[10,2048,64]{1,2,0:T(8,128)S(1)} fusion(bf16[10,2048,64]{1,2,0:T(8,128)(2,1)} %all_to_all.19, bf16[2048,2048]{1,0:T(8,128)(2,1)} %all-gather.8.cloned.1.call-done), kind=kOutput, calls=%fused_computation.29 | convolution fusion | flops 5368709120 | bytes 16252928 | tf_op jit(solution)/shard_map/jy,zyi->zji/dot_general | solution.py:70
  318.4 14.9 %fusion.78 = (bf16[10,2048,64]{1,2,0:T(8,128)(2,1)}, bf16[1,2048,64]{1,2,0:T(8,128)(2,1)S(1)}, f32[1,2048,64]{1,2,0:T(8,128)S(1)}, f32[1,2048,64]{1,2,0:T(8,128)...) fusion(f32[]{:T(128)S(6)} %neg.27, f32[]{:T(128)} %bitcast.9, ...), kind=kLoop, calls=%fused_computation.126 | loop fusion | flops 13631487 | bytes 8921456
  333.3 0.7 convert_dynamic-update-slice_fusion.8
  334.1 4.8 convert_dynamic-update-slice_fusion.7
  338.9 0.7 convert_dynamic-update-slice_fusion.6
  339.6 7.6 %convert_dynamic-update-slice_fusion.5 = bf16[10,2048,64]{1,2,0:T(8,128)(2,1)} fusion(bf16[10,2048,64]{1,2,0:T(8,128)(2,1)} %convert_dynamic-update-slice_fusion.6, f32[1,2048,64]{1,2,0:T(8,128)S(1)} %get-tuple-element.8, f32[1,2048,64]{1,2,0:T(8,128)S(1)} %get-tuple-element.5, f32[]{:T(128)} %bitcast.8, f32[]{:T(128)S(6)} %neg.27, f32[]{:T(128)} %bitcast.9, ...), kind=kLoop, calls=%fused_computation.132 | loop fusion | flops 4063232 | bytes 1324308
  347.2 0.7 convert_dynamic-update-slice_fusion.4
  348.0 10.4 %convert_dynamic-update-slice_fusion.3 = bf16[10,2048,64]{1,2,0:T(8,128)(2,1)} fusion(bf16[10,2048,64]{1,2,0:T(8,128)(2,1)} %convert_dynamic-update-slice_fusion.4, f32[1,2048,64]{1,2,0:T(8,128)S(1)} %get-tuple-element.7, f32[1,2048,64]{1,2,0:T(8,128)S(1)} %get-tuple-element.6, f32[]{:T(128)} %bitcast.8, f32[]{:T(128)S(6)} %neg.27, f32[]{:T(128)} %bitcast.9, ...), kind=kLoop, calls=%fused_computation.130 | loop fusion | flops 5636096 | bytes 1326364
  358.4 0.7 convert_dynamic-update-slice_fusion.2
  359.1 14.0 %convert_dynamic-update-slice_fusion.1 = bf16[10,2048,64]{1,2,0:T(8,128)(2,1)} fusion(bf16[10,2048,64]{1,2,0:T(8,128)(2,1)} %convert_dynamic-update-slice_fusion.2, f32[]{:T(128)} %bitcast.8, f32[]{:T(128)S(6)} %neg.27, f32[]{:T(128)} %bitcast.9, f32[]{:T(128)} %bitcast.10, f32[]{:T(128)S(6)} %neg.28, f32[]{:T(128)} %bitcast.11, f32[]{:T(128)} %bitcast.12, ...), kind=kLoop, calls=%fused_computation.128 | loop fusion | flops 8912896 | bytes 2377508
  373.1 14.0 %convert_dynamic-update-slice_fusion = bf16[10,2048,64]{1,2,0:T(8,128)(2,1)} fusion(bf16[10,2048,64]{1,2,0:T(8,128)(2,1)} %convert_dynamic-update-slice_fusion.1, f32[]{:T(128)} %bitcast.8, f32[]{:T(128)S(6)} %neg.27, f32[]{:T(128)} %bitcast.9, f32[]{:T(128)} %bitcast.10, f32[]{:T(128)S(6)} %neg.28, f32[]{:T(128)} %bitcast.11, f32[]{:T(128)} %bitcast.12, ...), kind=kLoop, calls=%fused_computation.127 | loop fusion | flops 8650752 | bytes 2377508 | tf_op jit(solution)/shard_map/stack | solution.py:43
  387.1 9.8 %fusion.15 = bf16[10,2048,64]{1,2,0:T(8,128)(2,1)S(1)} fusion(bf16[10,2048,64]{1,2,0:T(8,128)(2,1)} %convert_dynamic-update-slice_fusion, bf16[2048,2048]{1,0:T(8,128)(2,1)} %all-gather.10.cloned.1.call-done), kind=kOutput, calls=%fused_computation.31 | convolution fusion | flops 5370019840 | bytes 13631488 | tf_op jit(solution)/shard_map/yj,zji->zyi/dot_general | solution.py:79
  397.4 65.4 %all_to_all.23 = bf16[8,10,256,64]{2,3,1,0:T(8,128)(2,1)S(1)} all-to-all(bf16[8,10,256,64]{2,3,1,0:T(8,128)(2,1)S(1)} %fusion.70), channel_id=1, replica_groups=mesh['px'=4,'py'=8] {'py'}, dimensions={0} | all-to-all | bytes 5242880 | tf_op jit(solution)/shard_map/all_to_all | solution.py:86
  462.8 1.8 copy.22
  464.6 4.4 copy.23
  469.7 9.2 %select_bitcast_fusion = f32[1,10,256,512]{3,2,1,0:T(8,128)} fusion(s32[10,256,512]{2,1,0:T(8,128)} %param.21, f32[]{:T(128)} %bitcast.44, f32[]{:T(128)} %bitcast.43, f32[]{:T(128)} %bitcast.42, f32[]{:T(128)} %bitcast.41), kind=kLoop, calls=%fused_computation.28 | loop fusion | flops 10485760 | bytes 10485776 | tf_op jit(solution)/shard_map/stack | solution.py:106
  478.9 10.5 %slice_convert_fusion.1 = (f32[1,10,256,512]{3,2,1,0:T(8,128)}, f32[1,10,256,512]{3,2,1,0:T(8,128)}) fusion(s32[2,10,256,512]{3,2,1,0:T(8,128)} %param.22), kind=kLoop, calls=%fused_computation.27 | loop fusion | flops 2621440 | bytes 20971520 | tf_op jit(solution)/shard_map/convert_element_type | solution.py:110
  489.4 83.9 %all-gather.12.cloned.1.call-done = bf16[10,256,2048]{2,1,0:T(8,128)(2,1)} async-done(((bf16[10,256,512]{2,1,0:T(8,128)(2,1)}), bf16[10,256,2048]{2,1,0:T(8,128)(2,1)}) %all-gather.12.cloned.1.call-update) | async-done | bytes 10485776 | tf_op jit(solution)/shard_map/all_gather | solution.py:100
  573.3 8.5 %fusion.18 = f32[10,256,512]{2,1,0:T(8,128)S(1)} fusion(bf16[10,256,2048]{2,1,0:T(8,128)(2,1)} %all-gather.12.cloned.1.call-done, bf16[2048,512]{1,0:T(8,128)(2,1)S(1)} %copy-done.14), kind=kOutput, calls=%fused_computation.42 | convolution fusion | flops 5368709120 | bytes 17825792 | tf_op jit(solution)/shard_map/zyi,ix->zyx/dot_general | solution.py:98
  581.8 5.9 pad_maximum_fusion.4
  587.8 3.3 copy.24
  591.1 3.1 collective-permute-start
  594.2 3.3 copy.25
  597.5 2.2 collective-permute-start.1
  599.7 3.2 copy.26
  603.2 3.1 copy.27
  606.2 2.3 pad_maximum_fusion.10
  608.6 5.4 collective-permute-start.2
  613.9 1.9 collective-permute-start.3
  615.9 4.0 collective-permute-done.3
  619.9 27.9 %pad_maximum_fusion = f32[4,10,258,514]{3,2,1,0:T(8,128)} fusion(f32[4,10,1,514]{3,2,1,0:T(1,128)S(1)} %collective-permute-done.3, f32[4,10,256,1]{3,2,1,0:T(8,128)S(1)} %copy-done.8, f32[1,10,256,512]{3,2,1,0:T(8,128)} %get-tuple-element.19, f32[1,10,256,512]{3,2,1,0:T(8,128)S(1)} %bitcast.106, f32[1,10,256,512]{3,2,1,0:T(8,128)} %select_bitcast_fusion, ...), kind=kLoop, calls=%fused_computation | loop fusion | flops 37131360 | bytes 42435840 | tf_op jit(solution)/shard_map/concatenate | solution.py:16
  647.8 18.6 %slice_bitcast_fusion.3 = (f32[10,258,514]{2,1,0:T(8,128)}, f32[10,258,514]{2,1,0:T(8,128)}, f32[10,258,514]{2,1,0:T(8,128)}, f32[10,258,514]{2,1,0:T(8,128)}) fusion(f32[4,10,258,514]{3,2,1,0:T(8,128)} %pad_maximum_fusion), kind=kLoop, calls=%fused_computation.8 | loop fusion | bytes 42435840 | tf_op jit(solution)/shard_map/squeeze | solution.py:117
  666.4 14.9 %fusion.5 = f32[10,256,513]{2,1,0:T(8,128)} fusion(f32[10,258,514]{2,1,0:T(8,128)} %get-tuple-element.14, f32[10,258,514]{2,1,0:T(8,128)} %get-tuple-element.15, f32[10,258,514]{2,1,0:T(8,128)} %get-tuple-element.12, pred[513]{0:T(1024)(128)(4,1)S(1)} %fusion.81), kind=kLoop, calls=%fused_computation.11 | loop fusion | flops 6566400 | bytes 31519232 | tf_op jit(solution)/shard_map/jit(_where)/select_n | solution.py:122
  681.3 1.9 copy-done.3
  683.2 10.7 %fusion.7 = f32[10,257,512]{2,1,0:T(8,128)} fusion(f32[10,258,514]{2,1,0:T(8,128)S(1)} %copy-done.2, f32[10,258,514]{2,1,0:T(8,128)S(1)} %copy-done.3, f32[10,258,514]{2,1,0:T(8,128)} %get-tuple-element.13, pred[257]{0:T(512)(128)(4,1)S(1)} %fusion.84), kind=kLoop, calls=%fused_computation.16 | loop fusion | flops 6579200 | bytes 31580416 | tf_op jit(solution)/shard_map/jit(_where)/select_n | solution.py:131
  694.0 11.2 %fusion.8 = f32[10,256,512]{2,1,0:T(8,128)} fusion(f32[10,257,512]{2,1,0:T(8,128)} %fusion.7, f32[10,256,513]{2,1,0:T(8,128)} %fusion.5), kind=kLoop, calls=%fused_computation.20 | loop fusion | flops 3932160 | bytes 26214400 | tf_op jit(solution)/shard_map/add | solution.py:133
  (58 shorter events, 3.0 us)
Async XLA Ops:
  7.2 110.8 %copy-start = (bf16[2048,512]{1,0:T(8,128)(2,1)S(1)}, bf16[2048,512]{1,0:T(8,128)(2,1)}, u32[]{:S(2)}) copy-start(bf16[2048,512]{1,0:T(8,128)(2,1)} %param.17) | copy-start | bytes 6291460
  7.2 110.8 %all-gather.6.cloned.1.call-start = ((), (), s32[]{:S(2)}) async-start(), calls=%async_computation.2 | async-start | bytes 13107200 | tf_op jit(solution)/shard_map/all_gather | solution.py:64
  11.7 297.7 %all-gather.8.cloned.1.call-start = ((), (), s32[]{:S(2)}) async-start(), calls=%async_computation.3 | async-start | bytes 9437184 | tf_op jit(solution)/shard_map/all_gather | solution.py:72
  12.5 374.6 %all-gather.10.cloned.1.call-start = ((), (), s32[]{:S(2)}) async-start(), calls=%async_computation.4 | async-start | bytes 9437184 | tf_op jit(solution)/shard_map/all_gather | solution.py:81
  136.5 5.5 copy-start.11
  136.5 12.5 %copy-start.13 = (f32[256]{0:T(256)S(1)}, f32[256]{0:T(256)}, u32[]{:S(2)}) copy-start(f32[256]{0:T(256)} %param.14) | copy-start | bytes 3076
  136.5 134.4 %copy-start.10 = (f32[10]{0:T(128)S(1)}, f32[10]{0:T(128)}, u32[]{:S(2)}) copy-start(f32[10]{0:T(128)} %param.16) | copy-start | bytes 124
  136.5 161.9 %all-to-all-start = ((bf16[10,256,512]{1,0,2:T(8,128)(2,1)}), bf16[10,256,512]{1,0,2:T(8,128)(2,1)}, u32[]{:S(2)}, u32[]{:S(2)}) async-start(bf16[10,256,512]{1,0,2:T(8,128)(2,1)} %copy.19), calls=%async_computation | async-start | bytes 8388608 | tf_op jit(solution)/shard_map/all_to_all | solution.py:68
  142.0 431.3 %all-gather.12.cloned.1.call-start = ((), (), s32[]{:S(2)}) async-start(), calls=%async_computation.5 | async-start | bytes 13107200 | tf_op jit(solution)/shard_map/all_gather | solution.py:100
  464.6 4.4 copy-start.12
  478.9 94.4 %copy-start.14 = (bf16[2048,512]{1,0:T(8,128)(2,1)S(1)}, bf16[2048,512]{1,0:T(8,128)(2,1)}, u32[]{:S(2)}) copy-start(bf16[2048,512]{1,0:T(8,128)(2,1)} %param.20) | copy-start | bytes 6291460
  573.3 8.5 %copy-start.4 = (f32[1,10,256,512]{3,2,1,0:T(8,128)S(1)}, f32[1,10,256,512]{3,2,1,0:T(8,128)}, u32[]{:S(2)}) copy-start(f32[1,10,256,512]{3,2,1,0:T(8,128)} %get-tuple-element.18) | copy-start | bytes 15728644
  573.3 8.5 %copy-start.5 = (f32[1,10,256,512]{3,2,1,0:T(8,128)S(1)}, f32[1,10,256,512]{3,2,1,0:T(8,128)}, u32[]{:S(2)}) copy-start(f32[1,10,256,512]{3,2,1,0:T(8,128)} %get-tuple-element.19) | copy-start | bytes 15728644
  573.3 8.6 %copy-start.6 = (f32[1,10,256,512]{3,2,1,0:T(8,128)S(1)}, f32[1,10,256,512]{3,2,1,0:T(8,128)}, u32[]{:S(2)}) copy-start(f32[1,10,256,512]{3,2,1,0:T(8,128)} %select_bitcast_fusion) | copy-start | bytes 15728644
  581.7 6.0 copy-start.9
  591.1 8.6 %collective-permute-start = (f32[4,10,256,1]{2,0,3,1:T(4,128)S(1)}, f32[4,10,256,1]{2,0,3,1:T(4,128)S(1)}, u32[]{:S(2)}, u32[]{:S(2)}) collective-permute-start(f32[4,10,256,1]{2,0,3,1:T(4,128)S(1)} %copy.24), channel_id=1, source_target_pairs={{0,8},{8,16},{16,24},{1,9},{9,17},{17,25},{2,10},{10,18},{18,26},{... | collective-permute-start | bytes 122888 | tf_op jit(solution)/shard_map/ppermute | solution.py:12
  597.5 5.6 collective-permute-start.1
  603.2 16.8 %slice-start = ((s8[5242880]{0:T(1024)(128)(4,1)}), s8[1048576]{0:T(1024)(128)(4,1)S(1)}, s32[]{:S(2)}) async-start(s8[5242880]{0:T(1024)(128)(4,1)} %bitcast.105), calls=%async_computation.6 | async-start | bytes 2097152
  606.2 13.7 %slice-start.1 = ((s8[5242880]{0:T(1024)(128)(4,1)}), s8[4194304]{0:T(1024)(128)(4,1)S(1)}, s32[]{:S(2)}) async-start(s8[5242880]{0:T(1024)(128)(4,1)} %bitcast.105), calls=%async_computation.7 | async-start | bytes 8388608
  606.2 13.7 %copy-start.7 = (f32[4,10,256,1]{3,2,1,0:T(8,128)S(1)}, f32[4,10,256,1]{3,2,1,0:T(8,128)}, u32[]{:S(2)}) copy-start(f32[4,10,256,1]{3,2,1,0:T(8,128)} %copy.26) | copy-start | bytes 122884
  606.2 13.7 %copy-start.8 = (f32[4,10,256,1]{3,2,1,0:T(8,128)S(1)}, f32[4,10,256,1]{3,2,1,0:T(8,128)}, u32[]{:S(2)}) copy-start(f32[4,10,256,1]{3,2,1,0:T(8,128)} %copy.27) | copy-start | bytes 122884
  608.6 7.3 %collective-permute-start.2 = (f32[4,10,1,514]{3,2,1,0:T(1,128)S(1)}, f32[4,10,1,514]{3,2,1,0:T(1,128)S(1)}, u32[]{:S(2)}, u32[]{:S(2)}) collective-permute-start(f32[4,10,1,514]{3,2,1,0:T(1,128)S(1)} %get-tuple-element.10), channel_id=1, source_target_pairs={{0,1},{1,2},{2,3},{3,4},{4,5},{5,6},{6,7},{8,9},{9,10},{10,11},{11... | collective-permute-start | bytes 246728 | tf_op jit(solution)/shard_map/ppermute | solution.py:12
  613.9 6.0 collective-permute-start.3
  666.4 14.9 %copy-start.2 = (f32[10,258,514]{2,1,0:T(8,128)S(1)}, f32[10,258,514]{2,1,0:T(8,128)}, u32[]{:S(2)}) copy-start(f32[10,258,514]{2,1,0:T(8,128)} %get-tuple-element.14) | copy-start | bytes 15913444
  666.4 16.9 %copy-start.3 = (f32[10,258,514]{2,1,0:T(8,128)S(1)}, f32[10,258,514]{2,1,0:T(8,128)}, u32[]{:S(2)}) copy-start(f32[10,258,514]{2,1,0:T(8,128)} %get-tuple-element.15) | copy-start | bytes 15913444
  694.0 11.2 %copy-start.1 = (bf16[2048,512]{1,0:T(8,128)(2,1)S(1)}, bf16[2048,512]{1,0:T(8,128)(2,1)}, u32[]{:S(2)}) copy-start(bf16[2048,512]{1,0:T(8,128)(2,1)} %param.17) | copy-start | bytes 6291460
Sparse Core Ops, SparseCore 0:
  11.8 106.1 all-gather.5
  119.6 155.0 all-gather.7
  276.3 83.3 all-gather.9
  469.1 104.0 all-gather.11
